TPU v7x, 512 devices: a whole 4x8x8 slice. The times are simulated.
512 devices in a mesh: tm: 16 (over y_lo, x), space: 32 (over z, y_hi, core).
Axes of the slice: x: 4, y: 8 (y_hi: 2, y_lo: 4; y = y_hi * 4 + y_lo), z: 8, core: 2. Of those that a mesh axis runs over, the one named last changes fastest.
Arguments:
- frames: bfloat16 [16, 64, 96, 384], P('tm', 'space'), may hold values from -8 to 8
- cache_in: bfloat16 [2, 64, 96, 384], P(None, 'space'), may hold values from -6 to 6
- norm_gain: bfloat16 [384], replicated, may hold values from 0.5 to 1.5
- w_qkv: bfloat16 [384, 1152], replicated, may hold values from -0.5 to 0.5
- b_qkv: bfloat16 [1152], replicated, may hold values from -3 to 3
- w_proj: bfloat16 [384, 384], replicated, may hold values from -1.25 to 1.25
- b_proj: bfloat16 [384], replicated, may hold values from -2 to 2
- w_time: bfloat16 [3, 384, 768], replicated, may hold values from -0.1875 to 0.1875
- b_time: bfloat16 [768], replicated, may hold values from -3 to 3
- w_space: bfloat16 [3, 3, 384, 192], replicated, may hold values from -0.109375 to 0.109375
- b_space: bfloat16 [192], replicated, may hold values from -3 to 3
Outputs:
- decoded: bfloat16 [32, 128, 192, 192], P('tm', 'space')
All inputs are finite; a program needn't handle non-finite values.
Results may differ from a plain program's by a relative error of at most 0.01.
Values may be sent and summed in bfloat16 or wider, within the bound.
No kernel may reach another device: no remote copies, remote signals or barrier semaphores. Data moves between devices by JAX's collectives and lax.ppermute only.
A program may use at most 64 MiB of HBM per device.

v0:
```python
import jax
import jax.numpy as jnp
from jax import lax
from jax.sharding import PartitionSpec as P

EPSILON = 1e-06


def shifted(value, axis, steps):
    count = lax.axis_size(axis)
    leading, last = (max(0, -steps), min(count, count - steps))
    return lax.ppermute(value, axis, [(source, source + steps) for source in range(leading, last)])


def with_halo(block, sides, width):
    for axis, dim in sides:
        count = lax.axis_size(axis)
        forward = [(i, i + 1) for i in range(count - 1)]
        backward = [(target, source) for source, target in forward]
        low = lax.ppermute(
            lax.slice_in_dim(block, block.shape[dim] - width, None, axis=dim), axis, forward
        )
        high = lax.ppermute(lax.slice_in_dim(block, 0, width, axis=dim), axis, backward)
        block = jnp.concatenate([low, block, high], axis=dim)
    return block


def normalize(frames, norm_gain):
    widened = frames.astype(jnp.float32)
    inverse = lax.rsqrt(jnp.mean(widened * widened, axis=-1, keepdims=True) + EPSILON)
    return (widened * inverse * norm_gain.astype(jnp.float32)).astype(jnp.bfloat16)


def project(rows, weight, bias):
    return (
        jnp.dot(rows, weight, preferred_element_type=jnp.float32) + bias.astype(jnp.float32)
    ).astype(jnp.bfloat16)


def attend(running, queries, key_rows, value_rows):
    best, mass, total_sum = running
    scores = lax.dot_general(
        queries, key_rows, (((1,), (1,)), ((), ())), preferred_element_type=jnp.float32
    ) * queries.shape[1] ** (-0.5)
    new_best = jnp.maximum(best, jnp.max(scores, axis=1, keepdims=True))
    weights = jnp.exp(scores - new_best)
    mass = jnp.sum(weights, axis=1, keepdims=True)
    total_sum = jnp.dot(
        weights.astype(jnp.bfloat16), value_rows, preferred_element_type=jnp.float32
    )
    return (new_best, mass, total_sum)


def body(
    frames, cache_in, norm_gain, w_qkv, b_qkv, w_proj, b_proj, w_time, b_time, w_space, b_space
):
    channels = frames.shape[-1]
    rows = frames.shape[1]
    width = frames.shape[2]
    whole = lax.all_gather(frames.reshape(-1, channels), "space", axis=0, tiled=True)
    normed = normalize(frames, norm_gain).reshape(-1, channels)
    queries = project(normed, w_qkv[:, :channels], b_qkv[:channels])
    count = queries.shape[0]
    start_state = (
        jnp.full((count, 1), -1e30, jnp.float32),
        jnp.zeros((count, 1), jnp.float32),
        jnp.zeros((count, channels), jnp.float32),
    )
    normed_all = normalize(whole, norm_gain)
    key_rows = project(
        normed_all, w_qkv[:, channels : 2 * channels], b_qkv[channels : 2 * channels]
    )
    value_rows = project(normed_all, w_qkv[:, 2 * channels :], b_qkv[2 * channels :])
    final = attend(start_state, queries, key_rows, value_rows)
    mixed = (final[2] / final[1]).astype(jnp.bfloat16)
    hidden = (
        frames.reshape(-1, channels).astype(jnp.float32)
        + jnp.dot(mixed, w_proj, preferred_element_type=jnp.float32)
        + b_proj.astype(jnp.float32)
    ).astype(jnp.bfloat16)
    position = lax.axis_index("tm")
    carried = cache_in.reshape(2, -1, channels)
    near_frame = shifted(hidden, "tm", 1)
    near_frame = jnp.where(position == 0, carried[1], near_frame)
    far_frame = shifted(hidden, "tm", 2)
    far_frame = jnp.where(position == 1, carried[1], far_frame)
    far_frame = jnp.where(position == 0, carried[0], far_frame)
    timed = b_time.astype(jnp.float32) + jnp.dot(
        far_frame, w_time[0], preferred_element_type=jnp.float32
    )
    timed = timed + jnp.dot(near_frame, w_time[1], preferred_element_type=jnp.float32)
    timed = (timed + jnp.dot(hidden, w_time[2], preferred_element_type=jnp.float32)).astype(
        jnp.bfloat16
    )
    paired = jnp.stack([timed[:, :channels], timed[:, channels:]]).reshape(2, rows, width, channels)
    padded = with_halo(paired, (("space", 1),), 1)
    upsampled = jnp.repeat(jnp.repeat(padded, 2, axis=1)[:, 1 : 2 * rows + 3], 2, axis=2)
    upsampled = jnp.pad(upsampled, ((0, 0), (0, 0), (1, 1), (0, 0)))
    out_channels = w_space.shape[-1]
    result = jnp.zeros((8 * rows * width, out_channels), jnp.float32) + b_space.astype(jnp.float32)
    for row_tap in range(3):
        for col_tap in range(3):
            window = upsampled[
                :, row_tap : row_tap + 2 * rows, col_tap : col_tap + 2 * width
            ].reshape(-1, channels)
            result = result + jnp.dot(
                window, w_space[row_tap, col_tap], preferred_element_type=jnp.float32
            )
    return result.astype(jnp.bfloat16).reshape(2, 2 * rows, 2 * width, out_channels)


def solution(mesh):
    return jax.shard_map(
        body,
        mesh=mesh,
        in_specs=(
            P("tm", "space", None, None),
            P(None, "space", None, None),
            P(),
            P(),
            P(),
            P(),
            P(),
            P(),
            P(),
            P(),
            P(),
        ),
        out_specs=P("tm", "space", None, None),
        check_vma=False,
    )
```

profile of v0, /device:TPU:49, one launch (start us, length us, event | category | flops | bytes accessed | tf_op | source)
XLA Modules:
  0.0 203.1 jit_solution(68712272117767527)
XLA Ops:
  6.5 0.7 all-gather.2.cloned.1.call-update
  7.3 0.7 convert_element_type.67
  7.9 0.7 convert_element_type.79
  8.6 0.7 convert_element_type.64
  9.3 1.0 fusion.38
  10.3 0.8 slice_convert_fusion.1
  11.2 1.0 fusion.40
  12.2 1.0 fusion.67
  13.2 1.2 fusion.18
  14.4 108.0 %all-gather.2.cloned.1.call-done = bf16[6144,384]{1,0:T(8,128)(2,1)} async-done(((bf16[192,384]{1,0:T(8,128)(2,1)}), bf16[6144,384]{1,0:T(8,128)(2,1)}) %all-gather.2.cloned.1.call-update) | async-done | bytes 4718608 | tf_op jit(solution)/shard_map/all_gather | solution.py:60
  122.4 3.3 %fusion = f32[6144]{0:T(1024)S(1)} fusion(bf16[6144,384]{1,0:T(8,128)(2,1)} %all-gather.2.cloned.1.call-done), kind=kLoop, calls=%fused_computation.2 | loop fusion | flops 7071744 | bytes 4743168 | tf_op jit(solution)/shard_map/reduce_sum | solution.py:30
  125.8 8.1 %fusion.68 = (f32[192]{0:T(256)S(1)}, f32[192,6144]{1,0:T(8,128)}) fusion(bf16[192,384]{1,0:T(8,128)(2,1)S(1)} %fusion.18, f32[384]{0:T(512)S(1)} %get-tuple-element.22, bf16[6144,384]{1,0:T(8,128)(2,1)} %all-gather.2.cloned.1.call-done, f32[384]{0:T(512)S(1)} %convert_element_type.67, f32[6144]{0:T(1024)S(1)} %add_rsqrt_fusion, bf16[384,1152]{1,0:T(8,128)(2,1)} %param.14), kind=kOutput, calls=%fused_computation.90 | convolution fusion | flops 2734423808 | bytes 9907968 | tf_op jit(solution)/shard_map/dot_general | solution.py:42
  133.8 3.1 %fusion.3 = f32[192]{0:T(256)S(1)} fusion(f32[192,6144]{1,0:T(8,128)} %get-tuple-element.26, f32[192]{0:T(256)S(1)} %broadcast_maximum_fusion), kind=kLoop, calls=%fused_computation.9 | loop fusion | flops 2359104 | bytes 4720128 | tf_op jit(solution)/shard_map/reduce_sum | solution.py:47
  137.0 8.4 %fusion.25 = bf16[192,384]{1,0:T(8,128)(2,1)S(1)} fusion(f32[384]{0:T(512)S(1)} %get-tuple-element.24, bf16[6144,384]{1,0:T(8,128)(2,1)} %all-gather.2.cloned.1.call-done, f32[384]{0:T(512)S(1)} %convert_element_type.67, f32[6144]{0:T(1024)S(1)} %add_rsqrt_fusion, f32[192,6144]{1,0:T(8,128)} %get-tuple-element.26, f32[192]{0:T(256)S(1)} %broadcast_maximum_fusion, ...), kind=kOutput, calls=%fused_computation.33 | convolution fusion | flops 2734571520 | bytes 9908736 | tf_op jit(solution)/shard_map/dot_general | solution.py:48
  145.7 4.6 %collective-permute-start = (bf16[192,384]{1,0:T(8,128)(2,1)S(1)}, bf16[192,384]{1,0:T(8,128)(2,1)S(1)}, u32[]{:S(2)}, u32[]{:S(2)}) collective-permute-start(bf16[192,384]{1,0:T(8,128)(2,1)S(1)} %fusion.19), channel_id=1, source_target_pairs={{0,64},{32,96},{64,128},{96,160},{128,192},{160,224},{192,256},{22... | collective-permute-start | bytes 442376 | tf_op jit(solution)/shard_map/ppermute | solution.py:12
  150.3 2.2 %collective-permute-start.1 = (bf16[192,384]{1,0:T(8,128)(2,1)S(1)}, bf16[192,384]{1,0:T(8,128)(2,1)S(1)}, u32[]{:S(2)}, u32[]{:S(2)}) collective-permute-start(bf16[192,384]{1,0:T(8,128)(2,1)S(1)} %fusion.19), channel_id=1, source_target_pairs={{0,32},{32,64},{64,96},{96,128},{128,160},{160,192},{192,224},{224... | collective-permute-start | bytes 442376 | tf_op jit(solution)/shard_map/ppermute | solution.py:12
  152.8 2.3 %collective-permute-done = bf16[192,384]{1,0:T(8,128)(2,1)S(1)} collective-permute-done((bf16[192,384]{1,0:T(8,128)(2,1)S(1)}, bf16[192,384]{1,0:T(8,128)(2,1)S(1)}, u32[]{:S(2)}, u32[]{:S(2)}) %collective-permute-start) | collective-permute-done | bytes 147488 | tf_op jit(solution)/shard_map/ppermute | solution.py:12
  155.1 4.0 %collective-permute-done.1 = bf16[192,384]{1,0:T(8,128)(2,1)S(1)} collective-permute-done((bf16[192,384]{1,0:T(8,128)(2,1)S(1)}, bf16[192,384]{1,0:T(8,128)(2,1)S(1)}, u32[]{:S(2)}, u32[]{:S(2)}) %collective-permute-start.1) | collective-permute-done | bytes 147488 | tf_op jit(solution)/shard_map/ppermute | solution.py:12
  159.9 6.8 %collective-permute-start.2 = (bf16[2,1,96,384]{3,2,1,0:T(8,128)(2,1)S(1)}, bf16[2,1,96,384]{3,2,1,0:T(8,128)(2,1)S(1)}, u32[]{:S(2)}, u32[]{:S(2)}) collective-permute-start(bf16[2,1,96,384]{3,2,1,0:T(8,128)(2,1)S(1)} %get-tuple-element.14), channel_id=1, source_target_pairs={{0,1},{1,2},{2,3},{3,4},{4,5},{5,6},{6,7},{7,8},{8,9},{9,10},{10,1... | collective-permute-start | bytes 442376 | tf_op jit(solution)/shard_map/ppermute | solution.py:20
  166.7 2.1 %collective-permute-start.3 = (bf16[2,1,96,384]{3,2,1,0:T(8,128)(2,1)S(1)}, bf16[2,1,96,384]{3,2,1,0:T(8,128)(2,1)S(1)}, u32[]{:S(2)}, u32[]{:S(2)}) collective-permute-start(bf16[2,1,96,384]{3,2,1,0:T(8,128)(2,1)S(1)} %get-tuple-element.15), channel_id=1, source_target_pairs={{1,0},{2,1},{3,2},{4,3},{5,4},{6,5},{7,6},{8,7},{9,8},{10,9},{11,1... | collective-permute-start | bytes 442376 | tf_op jit(solution)/shard_map/ppermute | solution.py:23
  168.9 1.6 collective-permute-done.2
  170.4 8.7 %collective-permute-done.3 = bf16[2,1,96,384]{3,2,1,0:T(8,128)(2,1)S(1)} collective-permute-done((bf16[2,1,96,384]{3,2,1,0:T(8,128)(2,1)S(1)}, bf16[2,1,96,384]{3,2,1,0:T(8,128)(2,1)S(1)}, u32[]{:S(2)}, u32[]{:S(2)}) %collective-permute-start.3) | collective-permute-done | bytes 147488 | tf_op jit(solution)/shard_map/ppermute | solution.py:23
  179.5 2.3 %broadcast_in_dim.8 = bf16[2,6,96,2,384]{4,3,2,1,0:T(2,128)(2,1)} broadcast(bf16[2,6,96,384]{3,2,1,0:T(8,128)(2,1)S(1)} %slice.146), dimensions={0,1,2,4} | broadcast | bytes 2654208 | tf_op jit(solution)/shard_map/broadcast_in_dim | solution.py:97
  181.8 4.0 %reshape.92 = bf16[2,6,192,384]{3,2,1,0:T(8,128)(2,1)S(1)} reshape(bf16[2,6,96,2,384]{4,3,2,1,0:T(2,128)(2,1)} %broadcast_in_dim.8) | data formatting | bytes 3538944 | tf_op jit(solution)/shard_map/reshape | solution.py:97
  185.8 4.0 %pad_slice_fusion = (bf16[2,4,192,384]{3,2,1,0:T(8,128)(2,1)S(1)}, bf16[2,4,192,384]{3,2,1,0:T(8,128)(2,1)S(1)}, bf16[2,4,192,384]{3,2,1,0:T(8,128)(2,1)S(1)}, b...) fusion(bf16[2,6,192,384]{3,2,1,0:T(8,128)(2,1)S(1)} %reshape.92), kind=kLoop, calls=%fused_computation.34 | loop fusion | bytes 15925248 | tf_op jit(solution)/shard_map/slice | solution.py:103
  190.4 0.6 convolution_add_fusion.7
  191.0 0.6 convolution_add_fusion.6
  191.6 0.6 convolution_add_fusion.5
  192.2 0.6 convolution_add_fusion.4
  192.8 0.6 convolution_add_fusion.3
  193.4 0.6 convolution_add_fusion.2
  195.1 1.2 copy.13
  (28 shorter events, 3.4 us)
Async XLA Ops:
  6.5 138.9 %copy-start = (bf16[384,384]{1,0:T(8,128)(2,1)S(1)}, bf16[384,384]{1,0:T(8,128)(2,1)}, u32[]{:S(2)}) copy-start(bf16[384,384]{1,0:T(8,128)(2,1)} %param.16) | copy-start | bytes 884740
  6.5 115.9 %all-gather.2.cloned.1.call-start = ((), (), s32[]{:S(2)}) async-start(), calls=%async_computation | async-start | bytes 4866048 | tf_op jit(solution)/shard_map/all_gather | solution.py:60
  137.0 8.4 %copy-start.1 = (bf16[1,2,96,384]{3,2,1,0:T(8,128)(2,1)S(1)}, bf16[1,2,96,384]{3,2,1,0:T(8,128)(2,1)}, u32[]{:S(2)}) copy-start(bf16[1,2,96,384]{3,2,1,0:T(8,128)(2,1)} %param.11) | copy-start | bytes 442372
  137.0 15.5 %copy-start.2 = (bf16[3,384,768]{2,1,0:T(8,128)(2,1)S(1)}, bf16[3,384,768]{2,1,0:T(8,128)(2,1)}, u32[]{:S(2)}) copy-start(bf16[3,384,768]{2,1,0:T(8,128)(2,1)} %param.18) | copy-start | bytes 5308420
  145.7 9.4 %collective-permute-start = (bf16[192,384]{1,0:T(8,128)(2,1)S(1)}, bf16[192,384]{1,0:T(8,128)(2,1)S(1)}, u32[]{:S(2)}, u32[]{:S(2)}) collective-permute-start(bf16[192,384]{1,0:T(8,128)(2,1)S(1)} %fusion.19), channel_id=1, source_target_pairs={{0,64},{32,96},{64,128},{96,160},{128,192},{160,224},{192,256},{22... | collective-permute-start | bytes 442376 | tf_op jit(solution)/shard_map/ppermute | solution.py:12
  150.3 8.9 %collective-permute-start.1 = (bf16[192,384]{1,0:T(8,128)(2,1)S(1)}, bf16[192,384]{1,0:T(8,128)(2,1)S(1)}, u32[]{:S(2)}, u32[]{:S(2)}) collective-permute-start(bf16[192,384]{1,0:T(8,128)(2,1)S(1)} %fusion.19), channel_id=1, source_target_pairs={{0,32},{32,64},{64,96},{96,128},{128,160},{160,192},{192,224},{224... | collective-permute-start | bytes 442376 | tf_op jit(solution)/shard_map/ppermute | solution.py:12
  159.5 9.3 %copy-start.4 = (bf16[192]{0:T(256)(128)(2,1)S(1)}, bf16[192]{0:T(256)(128)(2,1)}, u32[]{:S(2)}) copy-start(bf16[192]{0:T(256)(128)(2,1)} %param.21) | copy-start | bytes 1156
  159.9 10.5 %collective-permute-start.2 = (bf16[2,1,96,384]{3,2,1,0:T(8,128)(2,1)S(1)}, bf16[2,1,96,384]{3,2,1,0:T(8,128)(2,1)S(1)}, u32[]{:S(2)}, u32[]{:S(2)}) collective-permute-start(bf16[2,1,96,384]{3,2,1,0:T(8,128)(2,1)S(1)} %get-tuple-element.14), channel_id=1, source_target_pairs={{0,1},{1,2},{2,3},{3,4},{4,5},{5,6},{6,7},{7,8},{8,9},{9,10},{10,1... | collective-permute-start | bytes 442376 | tf_op jit(solution)/shard_map/ppermute | solution.py:20
  166.7 12.4 %collective-permute-start.3 = (bf16[2,1,96,384]{3,2,1,0:T(8,128)(2,1)S(1)}, bf16[2,1,96,384]{3,2,1,0:T(8,128)(2,1)S(1)}, u32[]{:S(2)}, u32[]{:S(2)}) collective-permute-start(bf16[2,1,96,384]{3,2,1,0:T(8,128)(2,1)S(1)} %get-tuple-element.15), channel_id=1, source_target_pairs={{1,0},{2,1},{3,2},{4,3},{5,4},{6,5},{7,6},{8,7},{9,8},{10,9},{11,1... | collective-permute-start | bytes 442376 | tf_op jit(solution)/shard_map/ppermute | solution.py:23
  185.8 4.1 %copy-start.3 = (bf16[3,3,384,192]{2,3,1,0:T(8,128)(2,1)S(1)}, bf16[3,3,384,192]{2,3,1,0:T(8,128)(2,1)}, u32[]{:S(2)}) copy-start(bf16[3,3,384,192]{2,3,1,0:T(8,128)(2,1)} %param.20) | copy-start | bytes 3981316
Sparse Core Ops, SparseCore 0:
  10.7 111.6 all-gather.1
where the time goes:
time: 204 us; the launch traced here: 203 us
  waiting for transfers between devices  125 us (61%)
  matrix products  24.1 us (12%)
  starting transfers between devices  15.7 us (8%)
  between operations  13.7 us (7%)
  local copies, waits for them, and re-layouts  12.8 us (6%)
  other arithmetic  11.6 us (6%)
    all_gather x1, waiting for transfers between devices, body(): lax.all_gather(frames.reshape(-1, channels), 'space', axis=0, tiled=True)  108 us
    ppermute x1, waiting for transfers between devices, with_halo(): lax.ppermute(lax.slice_in_dim(block, 0, width, axis=dim), axis, backward)  8.74 us
    dot_general x1, matrix products, attend(): jnp.dot(weights.astype(jnp.bfloat16), value_rows, preferred_element_type=...  8.41 us
    dot_general x1, matrix products, attend(): lax.dot_general(queries, key_rows, (((1,), (1,)), ((), ())), preferred_el...  8.06 us
    ppermute x2, starting transfers between devices, shifted(): lax.ppermute(value, axis, [(source, source + steps) for source in range(l...  6.8 us
    ppermute x1, starting transfers between devices, with_halo(): lax.ppermute(lax.slice_in_dim(block, block.shape[dim] - width, None, axis...  6.78 us
    ppermute x2, waiting for transfers between devices, shifted(): lax.ppermute(value, axis, [(source, source + steps) for source in range(l...  6.31 us
    dot_general x9, matrix products, body(): jnp.dot(window, w_space[row_tap, col_tap], preferred_element_type=jnp.flo...  5.18 us
  transfers between devices with their start and end apart: 5, of which 5 were waited for; matrix products, arithmetic and copies ran while one was open for 4% of the time, Pallas kernels for 0%

commit v1 on v0

--- a/solution.py
+++ b/solution.py
@@ -57,7 +57,12 @@
     channels = frames.shape[-1]
     rows = frames.shape[1]
     width = frames.shape[2]
-    whole = lax.all_gather(frames.reshape(-1, channels), "space", axis=0, tiled=True)
+    whole = jnp.concatenate(
+        lax.all_to_all(
+            jnp.stack([frames.reshape(-1, channels)] * lax.axis_size("space")), "space", 0, 0
+        ),
+        axis=0,
+    )
     normed = normalize(frames, norm_gain).reshape(-1, channels)
     queries = project(normed, w_qkv[:, :channels], b_qkv[:channels])
     count = queries.shape[0]

time: 204 us -> 275 us (1.35)
  the two profiles are of different devices: /device:TPU:49 before, /device:TPU:81 now
where the time goes in v1:
time: 275 us; the launch traced here: 274 us
  waiting for transfers between devices  176 us (64%)
  starting transfers between devices  48 us (17%)
  matrix products  22.9 us (8%)
  local copies, waits for them, and re-layouts  15.7 us (6%)
  other arithmetic  11.6 us (4%)
    all_to_all x1, waiting for transfers between devices, body(): lax.all_to_all(jnp.stack([frames.reshape(-1, channels)] * lax.axis_size('...  162 us
    ppermute x1, starting transfers between devices, with_halo(): lax.ppermute(lax.slice_in_dim(block, block.shape[dim] - width, None, axis...  25 us
    all_to_all x1, starting transfers between devices, body(): lax.all_to_all(jnp.stack([frames.reshape(-1, channels)] * lax.axis_size('...  14.1 us
    dot_general x1, matrix products, attend(): jnp.dot(weights.astype(jnp.bfloat16), value_rows, preferred_element_type=...  8.37 us
    ppermute x1, waiting for transfers between devices, with_halo(): lax.ppermute(lax.slice_in_dim(block, 0, width, axis=dim), axis, backward)  8.23 us
    dot_general x1, matrix products, attend(): lax.dot_general(queries, key_rows, (((1,), (1,)), ((), ())), preferred_el...  7.89 us
    ppermute x2, starting transfers between devices, shifted(): lax.ppermute(value, axis, [(source, source + steps) for source in range(l...  6.89 us
    ppermute x2, waiting for transfers between devices, shifted(): lax.ppermute(value, axis, [(source, source + steps) for source in range(l...  5.52 us
  transfers between devices with their start and end apart: 5, of which 4 were waited for; matrix products, arithmetic and copies ran while one was open for 0% of the time, Pallas kernels for 0%

profile of v1, /device:TPU:81, one launch (start us, length us, event | category | flops | bytes accessed | tf_op | source)
XLA Modules:
  0.0 274.2 jit_solution(8093830139731514485)
XLA Ops:
  0.0 3.8 %stack.12 = bf16[32,192,384]{2,1,0:T(8,128)(2,1)} broadcast(bf16[192,384]{1,0:T(8,128)(2,1)} %bitcast.92), dimensions={1,2} | broadcast | bytes 4866048 | tf_op jit(solution)/shard_map/stack | solution.py:62
  3.9 14.1 %all-to-all-start = ((bf16[32,192,384]{2,1,0:T(8,128)(2,1)}), bf16[32,192,384]{2,1,0:T(8,128)(2,1)}, u32[]{:S(2)}, u32[]{:S(2)}) async-start(bf16[32,192,384]{2,1,0:T(8,128)(2,1)} %stack.12), calls=%async_computation | async-start | bytes 9437184 | tf_op jit(solution)/shard_map/all_to_all | solution.py:61
  18.4 0.2 fusion.12
  18.6 161.8 %all-to-all-done = bf16[32,192,384]{2,1,0:T(8,128)(2,1)} async-done(((bf16[32,192,384]{2,1,0:T(8,128)(2,1)}), bf16[32,192,384]{2,1,0:T(8,128)(2,1)}, u32[]{:S(2)}, u32[]{:S(2)}) %all-to-all-start) | async-done | bytes 4718624 | tf_op jit(solution)/shard_map/all_to_all | solution.py:61
  180.5 3.5 %multiply_reduce_fusion = f32[32,192]{1,0:T(8,128)S(1)} fusion(bf16[32,192,384]{2,1,0:T(8,128)(2,1)} %all-to-all-done), kind=kLoop, calls=%fused_computation.5 | loop fusion | flops 7071744 | bytes 4743168 | tf_op jit(solution)/shard_map/reduce_sum | solution.py:30
  184.1 4.5 %fusion.1 = bf16[6144,384]{1,0:T(8,128)(2,1)} fusion(f32[384]{0:T(512)S(1)} %convert_element_type.73, f32[6144]{0:T(1024)S(1)} %rsqrt.21, bf16[32,192,384]{2,1,0:T(8,128)(2,1)} %all-to-all-done), kind=kLoop, calls=%fused_computation.2 | loop fusion | flops 9437184 | bytes 9463296 | tf_op jit(solution)/shard_map/convert_element_type | solution.py:31
  188.6 7.9 %fusion.58 = (f32[192]{0:T(256)S(1)}, f32[192,6144]{1,0:T(8,128)}) fusion(bf16[192,384]{1,0:T(8,128)(2,1)S(1)} %fusion.12, bf16[6144,384]{1,0:T(8,128)(2,1)} %fusion.1, f32[384]{0:T(512)S(1)} %get-tuple-element.24, bf16[384,1152]{1,0:T(8,128)(2,1)S(1)} %copy-done.9), kind=kOutput, calls=%fused_computation.89 | convolution fusion | flops 2724986624 | bytes 9882368 | tf_op jit(solution)/shard_map/dot_general | solution.py:42
  196.5 3.1 %fusion.2 = f32[192]{0:T(256)S(1)} fusion(f32[192,6144]{1,0:T(8,128)} %get-tuple-element.26, f32[192]{0:T(256)S(1)} %broadcast_maximum_fusion), kind=kLoop, calls=%fused_computation.8 | loop fusion | flops 2359104 | bytes 4720128 | tf_op jit(solution)/shard_map/reduce_sum | solution.py:47
  199.6 8.4 %fusion.17 = bf16[192,384]{1,0:T(8,128)(2,1)S(1)} fusion(f32[192,6144]{1,0:T(8,128)} %get-tuple-element.26, f32[192]{0:T(256)S(1)} %broadcast_maximum_fusion, bf16[6144,384]{1,0:T(8,128)(2,1)} %fusion.1, f32[384]{0:T(512)S(1)} %get-tuple-element.22, bf16[384,1152]{1,0:T(8,128)(2,1)} %param.14, f32[192]{0:T(256)S(1)} %fusion.2), kind=kOutput, calls=%fused_computation.32 | convolution fusion | flops 2725134336 | bytes 9882624 | tf_op jit(solution)/shard_map/dot_general | solution.py:48
  208.2 4.7 %collective-permute-start = (bf16[192,384]{1,0:T(8,128)(2,1)S(1)}, bf16[192,384]{1,0:T(8,128)(2,1)S(1)}, u32[]{:S(2)}, u32[]{:S(2)}) collective-permute-start(bf16[192,384]{1,0:T(8,128)(2,1)S(1)} %fusion.13), channel_id=1, source_target_pairs={{0,64},{32,96},{64,128},{96,160},{128,192},{160,224},{192,256},{22... | collective-permute-start | bytes 442376 | tf_op jit(solution)/shard_map/ppermute | solution.py:12
  212.9 2.2 collective-permute-start.1
  215.1 0.3 fusion.20
  215.4 1.1 collective-permute-done
  216.5 4.5 %collective-permute-done.1 = bf16[192,384]{1,0:T(8,128)(2,1)S(1)} collective-permute-done((bf16[192,384]{1,0:T(8,128)(2,1)S(1)}, bf16[192,384]{1,0:T(8,128)(2,1)S(1)}, u32[]{:S(2)}, u32[]{:S(2)}) %collective-permute-start.1) | collective-permute-done | bytes 147488 | tf_op jit(solution)/shard_map/ppermute | solution.py:12
  221.0 0.3 fusion.22
  221.4 0.3 fusion.10
  221.8 25.0 %collective-permute-start.2 = (bf16[2,1,96,384]{3,2,1,0:T(8,128)(2,1)S(1)}, bf16[2,1,96,384]{3,2,1,0:T(8,128)(2,1)S(1)}, u32[]{:S(2)}, u32[]{:S(2)}) collective-permute-start(bf16[2,1,96,384]{3,2,1,0:T(8,128)(2,1)S(1)} %get-tuple-element.14), channel_id=1, source_target_pairs={{0,1},{1,2},{2,3},{3,4},{4,5},{5,6},{6,7},{7,8},{8,9},{9,10},{10,1... | collective-permute-start | bytes 442376 | tf_op jit(solution)/shard_map/ppermute | solution.py:20
  246.8 2.1 collective-permute-start.3
  248.9 8.2 %collective-permute-done.3 = bf16[2,1,96,384]{3,2,1,0:T(8,128)(2,1)S(1)} collective-permute-done((bf16[2,1,96,384]{3,2,1,0:T(8,128)(2,1)S(1)}, bf16[2,1,96,384]{3,2,1,0:T(8,128)(2,1)S(1)}, u32[]{:S(2)}, u32[]{:S(2)}) %collective-permute-start.3) | collective-permute-done | bytes 147488 | tf_op jit(solution)/shard_map/ppermute | solution.py:23
  257.4 2.3 broadcast_in_dim.8
  259.7 4.0 %reshape.105 = bf16[2,6,192,384]{3,2,1,0:T(8,128)(2,1)S(1)} reshape(bf16[2,6,96,2,384]{4,3,2,1,0:T(2,128)(2,1)} %broadcast_in_dim.8) | data formatting | bytes 3538944 | tf_op jit(solution)/shard_map/reshape | solution.py:102
  263.7 4.0 %pad_slice_fusion = (bf16[2,4,192,384]{3,2,1,0:T(8,128)(2,1)S(1)}, bf16[2,4,192,384]{3,2,1,0:T(8,128)(2,1)S(1)}, bf16[2,4,192,384]{3,2,1,0:T(8,128)(2,1)S(1)}, b...) fusion(bf16[2,6,192,384]{3,2,1,0:T(8,128)(2,1)S(1)} %reshape.105), kind=kLoop, calls=%fused_computation.33 | loop fusion | bytes 15925248 | tf_op jit(solution)/shard_map/slice | solution.py:108
  267.8 0.6 convolution_add_fusion.8
  268.3 0.6 convolution_add_fusion.7
  268.9 0.6 convolution_add_fusion.6
  269.5 0.6 convolution_add_fusion.5
  270.1 0.6 convolution_add_fusion.4
  270.7 0.6 convolution_add_fusion.3
  271.3 0.6 convolution_add_fusion.2
  271.8 0.6 convolution_add_fusion.1
  272.4 0.6 fusion.4
  273.0 1.2 copy.14
  (42 shorter events, 1.1 us)
Async XLA Ops:
  0.0 208.0 %copy-start = (bf16[384,384]{1,0:T(8,128)(2,1)S(1)}, bf16[384,384]{1,0:T(8,128)(2,1)}, u32[]{:S(2)}) copy-start(bf16[384,384]{1,0:T(8,128)(2,1)} %param.16) | copy-start | bytes 884740
  3.8 14.1 %copy-start.7 = (bf16[384]{0:T(512)(128)(2,1)S(1)}, bf16[384]{0:T(512)(128)(2,1)}, u32[]{:S(2)}) copy-start(bf16[384]{0:T(512)(128)(2,1)} %param.13) | copy-start | bytes 2308
  3.8 14.1 %copy-start.8 = (bf16[384]{0:T(512)(128)(2,1)S(1)}, bf16[384]{0:T(512)(128)(2,1)}, u32[]{:S(2)}) copy-start(bf16[384]{0:T(512)(128)(2,1)} %param.17) | copy-start | bytes 2308
  3.8 14.2 %copy-start.6 = (bf16[768]{0:T(1024)(128)(2,1)S(1)}, bf16[768]{0:T(1024)(128)(2,1)}, u32[]{:S(2)}) copy-start(bf16[768]{0:T(1024)(128)(2,1)} %param.19) | copy-start | bytes 4612
  3.9 14.2 %copy-start.1 = (bf16[1,2,96,384]{3,2,1,0:T(8,128)(2,1)S(1)}, bf16[1,2,96,384]{3,2,1,0:T(8,128)(2,1)}, u32[]{:S(2)}) copy-start(bf16[1,2,96,384]{3,2,1,0:T(8,128)(2,1)} %param.11) | copy-start | bytes 442372
  3.9 14.3 %copy-start.5 = (bf16[1152]{0:T(1024)(128)(2,1)S(1)}, bf16[1152]{0:T(1024)(128)(2,1)}, u32[]{:S(2)}) copy-start(bf16[1152]{0:T(1024)(128)(2,1)} %param.15) | copy-start | bytes 6916
  3.9 14.4 %copy-start.4 = (bf16[2,2,96,384]{3,2,1,0:T(8,128)(2,1)S(1)}, bf16[2,2,96,384]{3,2,1,0:T(8,128)(2,1)}, u32[]{:S(2)}) copy-start(bf16[2,2,96,384]{3,2,1,0:T(8,128)(2,1)} %param.12) | copy-start | bytes 884740
  3.9 14.5 %copy-start.9 = (bf16[384,1152]{1,0:T(8,128)(2,1)S(1)}, bf16[384,1152]{1,0:T(8,128)(2,1)}, u32[]{:S(2)}) copy-start(bf16[384,1152]{1,0:T(8,128)(2,1)} %param.14) | copy-start | bytes 2654212
  3.9 176.6 %all-to-all-start = ((bf16[32,192,384]{2,1,0:T(8,128)(2,1)}), bf16[32,192,384]{2,1,0:T(8,128)(2,1)}, u32[]{:S(2)}, u32[]{:S(2)}) async-start(bf16[32,192,384]{2,1,0:T(8,128)(2,1)} %stack.12), calls=%async_computation | async-start | bytes 9437184 | tf_op jit(solution)/shard_map/all_to_all | solution.py:61
  199.6 15.5 %copy-start.2 = (bf16[3,384,768]{2,1,0:T(8,128)(2,1)S(1)}, bf16[3,384,768]{2,1,0:T(8,128)(2,1)}, u32[]{:S(2)}) copy-start(bf16[3,384,768]{2,1,0:T(8,128)(2,1)} %param.18) | copy-start | bytes 5308420
  208.2 8.3 %collective-permute-start = (bf16[192,384]{1,0:T(8,128)(2,1)S(1)}, bf16[192,384]{1,0:T(8,128)(2,1)S(1)}, u32[]{:S(2)}, u32[]{:S(2)}) collective-permute-start(bf16[192,384]{1,0:T(8,128)(2,1)S(1)} %fusion.13), channel_id=1, source_target_pairs={{0,64},{32,96},{64,128},{96,160},{128,192},{160,224},{192,256},{22... | collective-permute-start | bytes 442376 | tf_op jit(solution)/shard_map/ppermute | solution.py:12
  212.9 8.1 %collective-permute-start.1 = (bf16[192,384]{1,0:T(8,128)(2,1)S(1)}, bf16[192,384]{1,0:T(8,128)(2,1)S(1)}, u32[]{:S(2)}, u32[]{:S(2)}) collective-permute-start(bf16[192,384]{1,0:T(8,128)(2,1)S(1)} %fusion.13), channel_id=1, source_target_pairs={{0,32},{32,64},{64,96},{96,128},{128,160},{160,192},{192,224},{224... | collective-permute-start | bytes 442376 | tf_op jit(solution)/shard_map/ppermute | solution.py:12
  221.4 27.5 %copy-start.10 = (bf16[192]{0:T(256)(128)(2,1)S(1)}, bf16[192]{0:T(256)(128)(2,1)}, u32[]{:S(2)}) copy-start(bf16[192]{0:T(256)(128)(2,1)} %param.21) | copy-start | bytes 1156
  221.8 27.1 %collective-permute-start.2 = (bf16[2,1,96,384]{3,2,1,0:T(8,128)(2,1)S(1)}, bf16[2,1,96,384]{3,2,1,0:T(8,128)(2,1)S(1)}, u32[]{:S(2)}, u32[]{:S(2)}) collective-permute-start(bf16[2,1,96,384]{3,2,1,0:T(8,128)(2,1)S(1)} %get-tuple-element.14), channel_id=1, source_target_pairs={{0,1},{1,2},{2,3},{3,4},{4,5},{5,6},{6,7},{7,8},{8,9},{9,10},{10,1... | collective-permute-start | bytes 442376 | tf_op jit(solution)/shard_map/ppermute | solution.py:20
  246.8 10.4 %collective-permute-start.3 = (bf16[2,1,96,384]{3,2,1,0:T(8,128)(2,1)S(1)}, bf16[2,1,96,384]{3,2,1,0:T(8,128)(2,1)S(1)}, u32[]{:S(2)}, u32[]{:S(2)}) collective-permute-start(bf16[2,1,96,384]{3,2,1,0:T(8,128)(2,1)S(1)} %get-tuple-element.15), channel_id=1, source_target_pairs={{1,0},{2,1},{3,2},{4,3},{5,4},{6,5},{7,6},{8,7},{9,8},{10,9},{11,1... | collective-permute-start | bytes 442376 | tf_op jit(solution)/shard_map/ppermute | solution.py:23
  263.7 4.0 %copy-start.3 = (bf16[3,3,384,192]{2,3,1,0:T(8,128)(2,1)S(1)}, bf16[3,3,384,192]{2,3,1,0:T(8,128)(2,1)}, u32[]{:S(2)}) copy-start(bf16[3,3,384,192]{2,3,1,0:T(8,128)(2,1)} %param.20) | copy-start | bytes 3981316
